TPU v7x, 32 devices: a whole 2x2x4 slice. The times are simulated.
32 devices in a mesh: seq: 4 (over y, x), batch: 8 (over z, core).
Axes of the slice: x: 2, y: 2, z: 4, core: 2. Of those that a mesh axis runs over, the one named last changes fastest.
Arguments:
- feats: bfloat16 [768, 4096], P('seq', 'batch'), parts along dimension 1, may hold values from -6 to 6
- qkv_weight: bfloat16 [768, 2304], replicated, may hold values from -0.21875 to 0.21875
- beta_weight: bfloat16 [768, 6], replicated, may hold values from -0.21875 to 0.21875
- beta_bias: float32 [6], replicated, may hold values from -7 to 0.5
- out_gain: float32 [768], replicated, may hold values from 0.1 to 1.9
Outputs:
- mixed: bfloat16 [4096, 768], P(('batch', 'seq')), parts along dimension 0
There are 8 independent parts, one for each index of `batch`. A program takes and returns all parts, laid end to end along the dimension named above; an argument that names none is the same for every part. Nothing has to cross between parts.
All inputs are finite; a program needn't handle non-finite values.
Results may differ from a plain program's by a relative error of at most 0.012.
Values may be sent and summed in bfloat16 or wider, within the bound.
No kernel may reach another device: no remote copies, remote signals or barrier semaphores. Data moves between devices by JAX's collectives and lax.ppermute only.
A program may use at most 64 MiB of HBM per device.

v0:
```python
import jax
import jax.numpy as jnp
from jax import lax
from jax.sharding import PartitionSpec as P

HEADS = 6
HD = 128
GROUP = 64
HIGHEST_ACCURACY = lax.Precision.HIGHEST


def entering(value, axis, join, neutral):
    count, mine = (lax.axis_size(axis), lax.axis_index(axis))
    pieces = jax.tree.map(lambda part: lax.all_gather(part, axis), value)
    running = jax.tree.map(
        lambda part, zero: jnp.full_like(part, 0) + jnp.asarray(zero, part.dtype), value, neutral
    )

    def turn(position, running):
        longer = join(running, jax.tree.map(lambda part: part[position], pieces))
        return jax.tree.map(lambda new, old: jnp.where(position < mine, new, old), longer, running)

    return lax.fori_loop(0, count - 1, turn, running)


def unit_inverse(gram):
    eye_block = jnp.eye(gram.shape[-1], dtype=jnp.float32)
    negated = -jnp.tril(gram, -1)
    inverse = eye_block + negated
    power = negated
    for level in range(5):
        power = jnp.einsum("nhij,nhjk->nhik", power, power, precision=HIGHEST_ACCURACY)
        inverse = inverse + jnp.einsum(
            "nhij,nhjk->nhik", inverse, power, precision=HIGHEST_ACCURACY
        )
    return inverse


def prepare(qkv, beta):
    rows = qkv.shape[0]
    blocks_count = rows // GROUP
    pieces = qkv.astype(jnp.float32).reshape(rows, 3, HEADS, HD)
    query = pieces[:, 0]
    keys = pieces[:, 1]
    values = pieces[:, 2]
    query = query * lax.rsqrt(jnp.sum(query * query, -1, keepdims=True) + 1e-06)
    keys = keys * lax.rsqrt(jnp.sum(keys * keys, -1, keepdims=True) + 1e-06)

    def blocks(arr):
        return arr.reshape(blocks_count, GROUP, HEADS, arr.shape[-1]).transpose(0, 2, 1, 3)

    query = blocks(query)
    keys = blocks(keys)
    values = blocks(values)
    rates = blocks(beta[:, :, None])
    weighted = keys * rates
    gram = jnp.einsum("nhik,nhjk->nhij", weighted, keys, precision=HIGHEST_ACCURACY)
    inverse = unit_inverse(gram)
    right = jnp.concatenate([weighted, values * rates], -1)
    solved = jnp.einsum("nhij,nhjk->nhik", inverse, right, precision=HIGHEST_ACCURACY)
    wfac = solved[..., :HD]
    ufac = solved[..., HD:]
    scores = jnp.tril(jnp.einsum("nhik,nhjk->nhij", query, keys, precision=HIGHEST_ACCURACY))
    return (query, keys, wfac, ufac, scores)


def finish(outputs, out_gain):
    rows = outputs.shape[0] * GROUP
    flat = outputs.transpose(0, 2, 1, 3).reshape(rows, HEADS, HD)
    power = jnp.mean(flat * flat, -1, keepdims=True) + 1e-06
    normed = flat * lax.rsqrt(power) * out_gain.reshape(HEADS, HD)
    return normed.reshape(rows, HEADS * HD).astype(jnp.bfloat16)


def compose(early, late):
    first_move, first_offset = early
    second_move, second_offset = late
    move = jnp.einsum("hij,hjk->hik", second_move, first_move, precision=HIGHEST_ACCURACY)
    offset = (
        jnp.einsum("hij,hjk->hik", second_move, first_offset, precision=HIGHEST_ACCURACY)
        + second_offset
    )
    return (move, offset)


def body(feats, qkv_weight, beta_weight, beta_bias, out_gain):
    local = lax.all_to_all(feats, "seq", split_axis=1, concat_axis=0, tiled=True)
    qkv = lax.dot_general(
        local, qkv_weight, (((0,), (0,)), ((), ())), preferred_element_type=jnp.float32
    ).astype(jnp.bfloat16)
    logits = lax.dot_general(
        local, beta_weight, (((0,), (0,)), ((), ())), preferred_element_type=jnp.float32
    )
    beta = jax.nn.sigmoid(logits + beta_bias)
    query, keys, wfac, ufac, scores = prepare(qkv, beta)
    eye_heads = jnp.broadcast_to(jnp.eye(HD, dtype=jnp.float32), (HEADS, HD, HD))
    empty = jnp.zeros((HEADS, HD, HD), jnp.float32)

    def first_pass(joint_matrix, item):
        query_block, key_block, weight_block, update_block, state_block = item
        held_value = jnp.einsum(
            "rnf,rfw->rnw", weight_block, joint_matrix, precision=HIGHEST_ACCURACY
        )
        carried_state = joint_matrix[..., HD:]
        residual_value = update_block - held_value[..., HD:]
        output_rows = jnp.einsum(
            "rnf,rfw->rnw", query_block, carried_state, precision=HIGHEST_ACCURACY
        ) + jnp.einsum("fco,fop->fcp", state_block, residual_value, precision=HIGHEST_ACCURACY)
        target_value = jnp.concatenate([-held_value[..., :HD], residual_value], -1)
        joint_matrix = joint_matrix + jnp.einsum(
            "mjr,mjz->mrz", key_block, target_value, precision=HIGHEST_ACCURACY
        )
        return (joint_matrix, output_rows)

    joint_start = jnp.concatenate([eye_heads, empty], -1)
    joint_matrix, local_out = lax.scan(first_pass, joint_start, (query, keys, wfac, ufac, scores))
    moves = joint_matrix[..., :HD]
    offsets = joint_matrix[..., HD:]
    prior = entering((moves, offsets), "seq", compose, (eye_heads, empty))
    incoming = prior[1]

    def second_pass(loop_carry, item):
        query_block, key_block, weight_block, state_block = item
        held_value = jnp.einsum(
            "rnf,rfw->rnw", weight_block, loop_carry, precision=HIGHEST_ACCURACY
        )
        output_rows = jnp.einsum(
            "rnf,rfw->rnw", query_block, loop_carry, precision=HIGHEST_ACCURACY
        ) - jnp.einsum("fco,fop->fcp", state_block, held_value, precision=HIGHEST_ACCURACY)
        loop_carry = loop_carry - jnp.einsum(
            "mjr,mjz->mrz", key_block, held_value, precision=HIGHEST_ACCURACY
        )
        return (loop_carry, output_rows)

    final_carry, added_out = lax.scan(second_pass, incoming, (query, keys, wfac, scores))
    return finish(local_out + added_out, out_gain)


def solution(mesh):
    placed = (P("seq", "batch"), P(), P(), P(), P())
    return jax.shard_map(
        body, mesh=mesh, in_specs=placed, out_specs=P(("batch", "seq"), None), check_vma=False
    )
```

profile of v0, /device:TPU:0, one launch (start us, length us, event | category | flops | bytes accessed | tf_op | source)
XLA Modules:
  0.0 174.5 jit_solution(12034097138395976783)
XLA Ops:
  6.5 1.8 %copy_bitcast_fusion = bf16[192,4,128]{2,0,1:T(8,128)(2,1)} fusion(bf16[192,512]{1,0:T(8,128)(2,1)} %param.11), kind=kLoop, calls=%fused_computation.83 | loop fusion | bytes 393216 | tf_op jit(solution)/shard_map/all_to_all | solution.py:87
  8.3 5.2 %all-to-all-start = ((bf16[192,4,128]{2,0,1:T(8,128)(2,1)}), bf16[192,4,128]{2,0,1:T(8,128)(2,1)}, u32[]{:S(2)}, u32[]{:S(2)}) async-start(bf16[192,4,128]{2,0,1:T(8,128)(2,1)} %copy_bitcast_fusion), calls=%async_computation | async-start | bytes 393216 | tf_op jit(solution)/shard_map/all_to_all | solution.py:87
  15.7 1.0 concatenate.9
  17.3 1.5 all-to-all-done
  18.8 2.6 %fusion.45 = f32[128,2304]{1,0:T(8,128)} fusion(bf16[768,128]{1,0:T(8,128)(2,1)} %bitcast.12, bf16[768,2304]{1,0:T(8,128)(2,1)S(1)} %copy-done), kind=kOutput, calls=%fused_computation.53 | convolution fusion | flops 453574656 | bytes 4915200 | tf_op jit(solution)/shard_map/dot_general | solution.py:88
  21.4 2.7 %copy.50 = f32[128,2304]{0,1:T(8,128)} copy(f32[128,2304]{1,0:T(8,128)} %fusion.45) | data formatting | bytes 2359296 | tf_op jit(solution)/shard_map/reshape | solution.py:42
  24.1 2.3 %multiply_reduce_fusion.1 = (f32[128,6]{0,1:T(8,128)S(1)}, f32[128,6]{0,1:T(8,128)S(1)}, f32[128,1,6,128]{0,3,2,1:T(8,128)}, f32[128,1,6,128]{0,3,2,1:T(8,128)}, f32[128,1,6,128]{0,3,2,1:T(8,128)}) fusion(f32[128,3,6,128]{0,3,2,1:T(8,128)} %bitcast.151), kind=kLoop, calls=%fused_computation.80 | loop fusion | flops 391680 | bytes 2365440 | tf_op jit(solution)/shard_map/reduce_sum | solution.py:46
  28.3 1.9 %copy.51 = f32[128,1,6,128]{3,0,2,1:T(8,128)} copy(f32[128,1,6,128]{0,3,2,1:T(8,128)} %get-tuple-element.311) | data formatting | bytes 786432 | tf_op jit(solution)/shard_map/slice | solution.py:44
  30.2 1.9 %copy.55 = f32[128,1,6,128]{3,0,2,1:T(8,128)} copy(f32[128,1,6,128]{0,3,2,1:T(8,128)} %get-tuple-element.310) | data formatting | bytes 786432 | tf_op jit(solution)/shard_map/slice | solution.py:45
  32.2 1.7 fusion.50
  33.9 1.4 reshape_broadcast_in_dim.3
  35.9 1.4 broadcast_multiply_fusion
  44.3 1.0 fusion.66
  46.0 1.9 %copy.57 = f32[128,1,6,128]{3,0,2,1:T(8,128)} copy(f32[128,1,6,128]{0,3,2,1:T(8,128)} %get-tuple-element.309) | data formatting | bytes 786432 | tf_op jit(solution)/shard_map/slice | solution.py:43
  48.0 1.2 multiply_bitcast_fusion
  50.0 1.5 convolution_select_fusion
  52.3 16.6 %while.38 = (s32[]{:T(128)}, f32[6,128,256]{2,1,0:T(8,128)}, f32[2,6,64,128]{3,2,1,0:T(8,128)}, f32[2,6,64,128]{3,2,1,0:T(8,128)}, f32[2,6,64,128]{3,2,1,0:T(8,1...) while((s32[]{:T(128)}, f32[6,128,256]{2,1,0:T(8,128)}, ...), condition=%wide.region_3.4_spmd, body=%wide.region_2.3_spmd.sunk | while | flops 415678464 | bytes 10029241 | solution.py:116
  52.3 1.9 %fusion.138 = f32[6,64,256]{2,1,0:T(8,128)S(1)} fusion(f32[6,128,256]{2,1,0:T(8,128)} %get-tuple-element.456, f32[2,6,64,128]{3,2,1,0:T(8,128)} %get-tuple-element.468, s32[]{:T(128)} %get-tuple-element.455), kind=kOutput, calls=%fused_computation.13.clone.1 | convolution fusion | flops 150994944 | bytes 1376768 | tf_op jit(solution)/shard_map/while/body/eval_jaxpr/rnf,rfw->rnw/dot_general | solution.py:101
  54.1 1.0 slice_negate_fusion.2
  55.2 1.5 fusion.139
  56.7 2.9 %convolution_add_fusion.10 = f32[6,128,256]{2,1,0:T(8,128)} fusion(f32[6,128,256]{2,1,0:T(8,128)} %get-tuple-element.456, f32[6,64,128]{2,1,0:T(8,128)S(1)} %get-tuple-element.432, f32[6,64,128]{2,1,0:T(8,128)S(1)} %get-tuple-element.433, f32[2,6,64,128]{3,2,1,0:T(8,128)S(1)} %copy-done.3, s32[]{:T(128)} %get-tuple-element.455), kind=kOutput, calls=%fused_computation.clone.1 | convolution fusion | flops 151289856 | bytes 2162692 | tf_op jit(solution)/shard_map/while/body/eval_jaxpr/mjr,mjz->mrz/dot_general | solution.py:110
  59.6 1.0 fusion.140
  60.6 1.9 %fusion.138 = f32[6,64,256]{2,1,0:T(8,128)S(1)} fusion(f32[6,128,256]{2,1,0:T(8,128)} %get-tuple-element.456, f32[2,6,64,128]{3,2,1,0:T(8,128)} %get-tuple-element.468, s32[]{:T(128)} %get-tuple-element.455), kind=kOutput, calls=%fused_computation.13.clone.1 | convolution fusion | flops 150994944 | bytes 1376768 | tf_op jit(solution)/shard_map/while/body/eval_jaxpr/rnf,rfw->rnw/dot_general | solution.py:101
  62.5 1.0 slice_negate_fusion.2
  63.5 1.5 fusion.139
  65.0 2.9 %convolution_add_fusion.10 = f32[6,128,256]{2,1,0:T(8,128)} fusion(f32[6,128,256]{2,1,0:T(8,128)} %get-tuple-element.456, f32[6,64,128]{2,1,0:T(8,128)S(1)} %get-tuple-element.432, f32[6,64,128]{2,1,0:T(8,128)S(1)} %get-tuple-element.433, f32[2,6,64,128]{3,2,1,0:T(8,128)S(1)} %copy-done.3, s32[]{:T(128)} %get-tuple-element.455), kind=kOutput, calls=%fused_computation.clone.1 | convolution fusion | flops 151289856 | bytes 2162692 | tf_op jit(solution)/shard_map/while/body/eval_jaxpr/mjr,mjz->mrz/dot_general | solution.py:110
  67.9 1.0 fusion.140
  68.9 2.1 %fusion.65 = (f32[6,128,128]{2,1,0:T(8,128)}, f32[6,128,128]{2,1,0:T(8,128)}) fusion(f32[6,128,256]{2,1,0:T(8,128)} %get-tuple-element.180), kind=kLoop, calls=%fused_computation.98 | loop fusion | bytes 1572864 | tf_op jit(solution)/shard_map/slice | solution.py:118
  71.8 30.7 %all-gather.5.cloned.1.call-done = f32[24,128,128]{2,1,0:T(8,128)} async-done(((f32[6,128,128]{2,1,0:T(8,128)}), f32[24,128,128]{2,1,0:T(8,128)}) %all-gather.5.cloned.1.call-update) | async-done | bytes 1572880 | tf_op jit(solution)/shard_map/all_gather | solution.py:14
  102.4 32.7 %all-gather.7.cloned.1.call-done = f32[24,128,128]{2,1,0:T(8,128)} async-done(((f32[6,128,128]{2,1,0:T(8,128)}), f32[24,128,128]{2,1,0:T(8,128)}) %all-gather.7.cloned.1.call-update) | async-done | bytes 1572880 | tf_op jit(solution)/shard_map/all_gather | solution.py:14
  135.1 10.2 %while.40 = (s32[]{:T(128)}, f32[6,128,128]{2,1,0:T(8,128)}, s32[]{:T(128)}, f32[4,6,128,128]{3,2,1,0:T(8,128)}, f32[4,6,128,128]{3,2,1,0:T(8,128)}, /*index=5*/s32[]{:T(128)}, s32[]{:T(128)}) while((s32[]{:T(128)}, f32[6,128,128]{2,1,0:T(8,128)}, s32[]{:T(128)}, f32[4,6,128,128]{3,2,1,0:T(8,128)}, f32[4,6,128,128]{3,2,1,0:T(8,128)}, ...), condition=%wide.region_5.6_spmd.clone, body=%wide.region_4.5_spmd.clone.sunk | while | flops 151388160 | bytes 2755167 | solution.py:23
  135.1 1.0 copy.105
  136.1 2.4 %fusion.154 = f32[6,128,128]{2,1,0:T(8,128)} fusion(f32[6,128,128]{2,1,0:T(8,128)S(1)} %copy.105, f32[4,6,128,128]{3,2,1,0:T(8,128)} %get-tuple-element.491, s32[]{:T(128)} %get-tuple-element.480, f32[4,6,128,128]{3,2,1,0:T(8,128)} %get-tuple-element.490, pred[]{:T(512)S(6)} %compare.4, pred[]{:T(512)S(6)} %lt.30), kind=kOutput, calls=%fused_computation.44.clone.1 | convolution fusion | flops 151388160 | bytes 1968640 | tf_op jit(solution)/shard_map/while/body/eval_jaxpr/hij,hjk->hik/dot_general | solution.py:80
  138.5 1.0 copy.105
  139.5 2.4 %fusion.154 = f32[6,128,128]{2,1,0:T(8,128)} fusion(f32[6,128,128]{2,1,0:T(8,128)S(1)} %copy.105, f32[4,6,128,128]{3,2,1,0:T(8,128)} %get-tuple-element.491, s32[]{:T(128)} %get-tuple-element.480, f32[4,6,128,128]{3,2,1,0:T(8,128)} %get-tuple-element.490, pred[]{:T(512)S(6)} %compare.4, pred[]{:T(512)S(6)} %lt.30), kind=kOutput, calls=%fused_computation.44.clone.1 | convolution fusion | flops 151388160 | bytes 1968640 | tf_op jit(solution)/shard_map/while/body/eval_jaxpr/hij,hjk->hik/dot_general | solution.py:80
  141.9 1.0 copy.105
  142.9 2.4 %fusion.154 = f32[6,128,128]{2,1,0:T(8,128)} fusion(f32[6,128,128]{2,1,0:T(8,128)S(1)} %copy.105, f32[4,6,128,128]{3,2,1,0:T(8,128)} %get-tuple-element.491, s32[]{:T(128)} %get-tuple-element.480, f32[4,6,128,128]{3,2,1,0:T(8,128)} %get-tuple-element.490, pred[]{:T(512)S(6)} %compare.4, pred[]{:T(512)S(6)} %lt.30), kind=kOutput, calls=%fused_computation.44.clone.1 | convolution fusion | flops 151388160 | bytes 1968640 | tf_op jit(solution)/shard_map/while/body/eval_jaxpr/hij,hjk->hik/dot_general | solution.py:80
  146.1 13.8 %while.39 = (s32[]{:T(128)}, f32[6,128,128]{2,1,0:T(8,128)}, f32[2,6,64,128]{3,2,1,0:T(8,128)}, f32[2,6,64,128]{3,2,1,0:T(8,128)}, f32[2,6,64,128]{3,2,1,0:T(8,1...) while((s32[]{:T(128)}, f32[6,128,128]{2,1,0:T(8,128)}, ...), condition=%wide.region_7.8_spmd, body=%wide.region_6.7_spmd.sunk | while | flops 264388608 | bytes 9046217 | solution.py:135
  146.1 1.6 fusion.149
  147.8 1.6 fusion.150
  150.5 2.6 %convolution_subtract_fusion.3 = f32[6,128,128]{2,1,0:T(8,128)} fusion(f32[6,128,128]{2,1,0:T(8,128)} %get-tuple-element.503, f32[6,64,128]{2,1,0:T(8,128)S(1)} %fusion.149, f32[2,6,64,128]{3,2,1,0:T(8,128)S(1)} %copy-done.4, s32[]{:T(128)} %get-tuple-element.502), kind=kOutput, calls=%fused_computation.25.clone.1 | convolution fusion | flops 75595776 | bytes 1179652 | tf_op jit(solution)/shard_map/while/body/eval_jaxpr/mjr,mjz->mrz/dot_general | solution.py:130
  153.0 1.6 fusion.149
  154.7 1.6 fusion.150
  157.4 2.6 %convolution_subtract_fusion.3 = f32[6,128,128]{2,1,0:T(8,128)} fusion(f32[6,128,128]{2,1,0:T(8,128)} %get-tuple-element.503, f32[6,64,128]{2,1,0:T(8,128)S(1)} %fusion.149, f32[2,6,64,128]{3,2,1,0:T(8,128)S(1)} %copy-done.4, s32[]{:T(128)} %get-tuple-element.502), kind=kOutput, calls=%fused_computation.25.clone.1 | convolution fusion | flops 75595776 | bytes 1179652 | tf_op jit(solution)/shard_map/while/body/eval_jaxpr/mjr,mjz->mrz/dot_general | solution.py:130
  160.0 1.9 %multiply_reduce_fusion = (f32[2,64,6]{1,2,0:T(8,128)S(1)}, f32[2,64,6,128]{3,1,2,0:T(8,128)}) fusion(f32[2,6,64,128]{3,2,1,0:T(8,128)} %get-tuple-element.179, f32[2,6,64,128]{3,2,1,0:T(8,128)} %get-tuple-element.182), kind=kLoop, calls=%fused_computation.77 | loop fusion | flops 294144 | bytes 1182720 | tf_op jit(solution)/shard_map/reduce_sum | solution.py:70
  162.8 1.9 %copy.63 = f32[128,768]{1,0:T(8,128)} copy(f32[128,768]{0,1:T(8,128)} %bitcast.156) | data formatting | bytes 786432 | tf_op jit(solution)/shard_map/mul | solution.py:71
  164.7 1.2 copy.61
  165.9 1.8 %fusion.56 = bf16[128,768]{1,0:T(8,128)(2,1)} fusion(f32[128,768]{1,0:T(8,128)} %copy.63, f32[16,8,6,128]{3,2,1,0:T(8,128)S(1)} %bitcast.154, f32[768]{0:T(1024)S(1)} %copy-done.12), kind=kLoop, calls=%fused_computation.73 | loop fusion | flops 294912 | bytes 986112 | tf_op jit(solution)/shard_map/convert_element_type | solution.py:72
  (77 shorter events, 19.3 us)
Async XLA Ops:
  6.5 12.3 %copy-start = (bf16[768,2304]{1,0:T(8,128)(2,1)S(1)}, bf16[768,2304]{1,0:T(8,128)(2,1)}, u32[]{:S(2)}) copy-start(bf16[768,2304]{1,0:T(8,128)(2,1)} %param.12) | copy-start | bytes 10616836
  8.3 10.5 %all-to-all-start = ((bf16[192,4,128]{2,0,1:T(8,128)(2,1)}), bf16[192,4,128]{2,0,1:T(8,128)(2,1)}, u32[]{:S(2)}, u32[]{:S(2)}) async-start(bf16[192,4,128]{2,0,1:T(8,128)(2,1)} %copy_bitcast_fusion), calls=%async_computation | async-start | bytes 393216 | tf_op jit(solution)/shard_map/all_to_all | solution.py:87
  13.5 88.9 %all-gather.5.cloned.1.call-start = ((), (), s32[]{:S(2)}) async-start(), calls=%async_computation.1 | async-start | bytes 1966080 | tf_op jit(solution)/shard_map/all_gather | solution.py:14
  35.2 2.1 %copy-start.11 = (pred[64,64]{1,0:T(8,128)(4,1)S(1)}, pred[64,64]{1,0:T(8,128)(4,1)}, u32[]{:S(2)}) copy-start(pred[64,64]{1,0:T(8,128)(4,1)} %iota_compare_fusion.2) | copy-start | bytes 12292
  37.3 1.9 %copy-start.1 = (f32[2,6,64,128]{3,2,1,0:T(8,128)}, f32[2,6,64,128]{3,2,1,0:T(8,128)S(1)}, u32[]{:S(2)}) copy-start(f32[2,6,64,128]{3,2,1,0:T(8,128)S(1)} %get-tuple-element.497) | copy-start | bytes 1179652
  37.3 1.9 %copy-start.10 = (f32[64,64]{1,0:T(8,128)S(1)}, f32[64,64]{1,0:T(8,128)}, u32[]{:S(2)}) copy-start(f32[64,64]{1,0:T(8,128)} %fusion.61) | copy-start | bytes 49156
  48.0 2.0 %copy-start.2 = (f32[2,6,64,128]{3,2,1,0:T(8,128)S(1)}, f32[2,6,64,128]{3,2,1,0:T(8,128)}, u32[]{:S(2)}) copy-start(f32[2,6,64,128]{3,2,1,0:T(8,128)} %copy-done.1) | copy-start | bytes 1179652
  52.3 2.9 %copy-start.5 = (f32[2,6,64,128]{3,2,1,0:T(8,128)S(1)}, f32[2,6,64,128]{3,2,1,0:T(8,128)}, u32[]{:S(2)}) copy-start(f32[2,6,64,128]{3,2,1,0:T(8,128)} %get-tuple-element.470) | copy-start | bytes 1179652 | tf_op jit(solution)/shard_map/while
  52.3 4.4 %copy-start.3 = (f32[2,6,64,128]{3,2,1,0:T(8,128)S(1)}, f32[2,6,64,128]{3,2,1,0:T(8,128)}, u32[]{:S(2)}) copy-start(f32[2,6,64,128]{3,2,1,0:T(8,128)} %get-tuple-element.467) | copy-start | bytes 1179652 | tf_op jit(solution)/shard_map/while
  55.1 4.4 %copy-start.6 = (f32[2,6,64,64]{3,2,1,0:T(8,128)S(1)}, f32[2,6,64,64]{3,2,1,0:T(8,128)}, u32[]{:S(2)}) copy-start(f32[2,6,64,64]{3,2,1,0:T(8,128)} %get-tuple-element.471) | copy-start | bytes 589828 | tf_op jit(solution)/shard_map/while
  60.6 2.9 %copy-start.5 = (f32[2,6,64,128]{3,2,1,0:T(8,128)S(1)}, f32[2,6,64,128]{3,2,1,0:T(8,128)}, u32[]{:S(2)}) copy-start(f32[2,6,64,128]{3,2,1,0:T(8,128)} %get-tuple-element.470) | copy-start | bytes 1179652 | tf_op jit(solution)/shard_map/while
  60.6 4.4 %copy-start.3 = (f32[2,6,64,128]{3,2,1,0:T(8,128)S(1)}, f32[2,6,64,128]{3,2,1,0:T(8,128)}, u32[]{:S(2)}) copy-start(f32[2,6,64,128]{3,2,1,0:T(8,128)} %get-tuple-element.467) | copy-start | bytes 1179652 | tf_op jit(solution)/shard_map/while
  63.4 4.4 %copy-start.6 = (f32[2,6,64,64]{3,2,1,0:T(8,128)S(1)}, f32[2,6,64,64]{3,2,1,0:T(8,128)}, u32[]{:S(2)}) copy-start(f32[2,6,64,64]{3,2,1,0:T(8,128)} %get-tuple-element.471) | copy-start | bytes 589828 | tf_op jit(solution)/shard_map/while
  71.0 64.1 %all-gather.7.cloned.1.call-start = ((), (), s32[]{:S(2)}) async-start(), calls=%async_computation.2 | async-start | bytes 1966080 | tf_op jit(solution)/shard_map/all_gather | solution.py:14
  146.1 3.2 %copy-start.7 = (f32[2,6,64,64]{3,2,1,0:T(8,128)S(1)}, f32[2,6,64,64]{3,2,1,0:T(8,128)}, u32[]{:S(2)}) copy-start(f32[2,6,64,64]{3,2,1,0:T(8,128)} %get-tuple-element.516) | copy-start | bytes 589828 | tf_op jit(solution)/shard_map/while
  146.1 3.3 %copy-start.8 = (f32[2,6,64,128]{3,2,1,0:T(8,128)S(1)}, f32[2,6,64,128]{3,2,1,0:T(8,128)}, u32[]{:S(2)}) copy-start(f32[2,6,64,128]{3,2,1,0:T(8,128)} %get-tuple-element.504) | copy-start | bytes 1179652 | tf_op jit(solution)/shard_map/while
  146.1 4.3 %copy-start.4 = (f32[2,6,64,128]{3,2,1,0:T(8,128)S(1)}, f32[2,6,64,128]{3,2,1,0:T(8,128)}, u32[]{:S(2)}) copy-start(f32[2,6,64,128]{3,2,1,0:T(8,128)} %get-tuple-element.513) | copy-start | bytes 1179652 | tf_op jit(solution)/shard_map/while
  149.7 0.8 copy-start.9
  153.0 3.2 %copy-start.7 = (f32[2,6,64,64]{3,2,1,0:T(8,128)S(1)}, f32[2,6,64,64]{3,2,1,0:T(8,128)}, u32[]{:S(2)}) copy-start(f32[2,6,64,64]{3,2,1,0:T(8,128)} %get-tuple-element.516) | copy-start | bytes 589828 | tf_op jit(solution)/shard_map/while
  153.0 3.3 %copy-start.8 = (f32[2,6,64,128]{3,2,1,0:T(8,128)S(1)}, f32[2,6,64,128]{3,2,1,0:T(8,128)}, u32[]{:S(2)}) copy-start(f32[2,6,64,128]{3,2,1,0:T(8,128)} %get-tuple-element.504) | copy-start | bytes 1179652 | tf_op jit(solution)/shard_map/while
  153.0 4.3 %copy-start.4 = (f32[2,6,64,128]{3,2,1,0:T(8,128)S(1)}, f32[2,6,64,128]{3,2,1,0:T(8,128)}, u32[]{:S(2)}) copy-start(f32[2,6,64,128]{3,2,1,0:T(8,128)} %get-tuple-element.513) | copy-start | bytes 1179652 | tf_op jit(solution)/shard_map/while
  156.6 0.8 copy-start.9
  160.0 6.0 %copy-start.12 = (f32[768]{0:T(1024)S(1)}, f32[768]{0:T(1024)}, u32[]{:S(2)}) copy-start(f32[768]{0:T(1024)} %param.15) | copy-start | bytes 9220
Sparse Core Ops, SparseCore 0:
  71.1 31.2 all-gather.4
  104.3 30.8 all-gather.6
where the time goes:
time: 176 us; the launch traced here: 175 us
  waiting for transfers between devices  65.4 us (37%)
  matrix products  46.7 us (27%)
  local copies, waits for them, and re-layouts  30.2 us (17%)
  between operations  13.6 us (8%)
  other arithmetic  13 us (7%)
  starting transfers between devices  5.42 us (3%)
    all_gather x2, waiting for transfers between devices, entering(): pieces = jax.tree.map(lambda part: lax.all_gather(part, axis), value)  63.4 us
    dot_general x3, matrix products, compose(): jnp.einsum('hij,hjk->hik', second_move, first_offset, precision=HIGHEST_A...  7.21 us
    dot_general x2, matrix products, first_pass(): jnp.einsum('mjr,mjz->mrz', key_block, target_value, precision=HIGHEST_ACC...  5.78 us
    all_to_all x1, starting transfers between devices, body(): lax.all_to_all(feats, 'seq', split_axis=1, concat_axis=0, tiled=True)  5.19 us
    dot_general x2, matrix products, second_pass(): jnp.einsum('mjr,mjz->mrz', key_block, held_value, precision=HIGHEST_ACCUR...  5.12 us
    while x31, local copies, waits for them, and re-layouts  4.53 us
    dot_general x2, matrix products, first_pass(): jnp.einsum('rnf,rfw->rnw', weight_block, joint_matrix, precision=HIGHEST_...  3.72 us
  transfers between devices with their start and end apart: 3, of which 3 were waited for; matrix products, arithmetic and copies ran while one was open for 2% of the time, Pallas kernels for 0%

commit v1 on v0

--- a/solution.py
+++ b/solution.py
@@ -84,7 +84,10 @@
 
 
 def body(feats, qkv_weight, beta_weight, beta_bias, out_gain):
-    local = lax.all_to_all(feats, "seq", split_axis=1, concat_axis=0, tiled=True)
+    local = jnp.concatenate(
+        lax.all_to_all(jnp.stack(jnp.split(feats, lax.axis_size("seq"), axis=1)), "seq", 0, 0),
+        axis=0,
+    )
     qkv = lax.dot_general(
         local, qkv_weight, (((0,), (0,)), ((), ())), preferred_element_type=jnp.float32
     ).astype(jnp.bfloat16)

time: 176 us -> 173 us (0.983)
  local copies, waits for them, and re-layouts: 30.2 us -> 28.1 us
    all_to_all x1 -> x0, local copies, waits for them, and re-layouts: 1.79 us -> none  [body(): lax.all_to_all(feats, 'seq', split_axis=1, concat_axis=0, tiled=True)]
  transfers between devices with their start and end apart: 3 -> 3, of which waited for: 3 -> 3; matrix products, arithmetic and copies ran while one was open for 2% -> 3% of each run, Pallas kernels for 0% -> 0%
where the time goes in v1:
time: 173 us; the launch traced here: 172 us
  waiting for transfers between devices  65.4 us (38%)
  matrix products  46 us (27%)
  local copies, waits for them, and re-layouts  28.1 us (16%)
  between operations  13.6 us (8%)
  other arithmetic  13.3 us (8%)
  starting transfers between devices  5.42 us (3%)
    all_gather x2, waiting for transfers between devices, entering(): pieces = jax.tree.map(lambda part: lax.all_gather(part, axis), value)  64 us
    dot_general x3, matrix products, compose(): jnp.einsum('hij,hjk->hik', second_move, first_offset, precision=HIGHEST_A...  7.23 us
    dot_general x2, matrix products, first_pass(): jnp.einsum('mjr,mjz->mrz', key_block, target_value, precision=HIGHEST_ACC...  5.78 us
    all_to_all x1, starting transfers between devices, body(): lax.all_to_all(jnp.stack(jnp.split(feats, lax.axis_size('seq'), axis=1)),...  5.19 us
    dot_general x2, matrix products, second_pass(): jnp.einsum('mjr,mjz->mrz', key_block, held_value, precision=HIGHEST_ACCUR...  5.13 us
    while x31, local copies, waits for them, and re-layouts  4.54 us
    dot_general x2, matrix products, first_pass(): jnp.einsum('rnf,rfw->rnw', weight_block, joint_matrix, precision=HIGHEST_...  3.72 us
  transfers between devices with their start and end apart: 3, of which 3 were waited for; matrix products, arithmetic and copies ran while one was open for 3% of the time, Pallas kernels for 0%

profile of v1, /device:TPU:0, one launch (start us, length us, event | category | flops | bytes accessed | tf_op | source)
XLA Modules:
  0.0 172.0 jit_solution(11951028394643286616)
XLA Ops:
  6.5 1.0 slice_bitcast_fusion.3
  8.3 5.2 %all-to-all-start = ((bf16[4,192,128]{2,1,0:T(8,128)(2,1)}), bf16[4,192,128]{2,1,0:T(8,128)(2,1)}, u32[]{:S(2)}, u32[]{:S(2)}) async-start(bf16[4,192,128]{2,1,0:T(8,128)(2,1)} %pad_maximum_fusion), calls=%async_computation | async-start | bytes 393216 | tf_op jit(solution)/shard_map/all_to_all | solution.py:88
  15.4 0.9 broadcast_in_dim.32
  16.3 1.0 concatenate.9
  17.8 0.9 all-to-all-done
  18.8 2.6 %fusion.45 = f32[128,2304]{1,0:T(8,128)} fusion(bf16[768,128]{1,0:T(8,128)(2,1)} %bitcast.15, bf16[768,2304]{1,0:T(8,128)(2,1)S(1)} %copy-done), kind=kOutput, calls=%fused_computation.53 | convolution fusion | flops 453574656 | bytes 4915200 | tf_op jit(solution)/shard_map/dot_general | solution.py:91
  21.4 2.7 %copy.34 = f32[128,2304]{0,1:T(8,128)} copy(f32[128,2304]{1,0:T(8,128)} %fusion.45) | data formatting | bytes 2359296 | tf_op jit(solution)/shard_map/reshape | solution.py:42
  24.1 2.3 %multiply_reduce_fusion.1 = (f32[128,6]{0,1:T(8,128)S(1)}, f32[128,6]{0,1:T(8,128)S(1)}, f32[128,1,6,128]{0,3,2,1:T(8,128)}, f32[128,1,6,128]{0,3,2,1:T(8,128)}, f32[128,1,6,128]{0,3,2,1:T(8,128)}) fusion(f32[128,3,6,128]{0,3,2,1:T(8,128)} %bitcast.152), kind=kLoop, calls=%fused_computation.80 | loop fusion | flops 391680 | bytes 2365440 | tf_op jit(solution)/shard_map/reduce_sum | solution.py:46
  27.0 1.9 %copy.35 = f32[128,1,6,128]{3,0,2,1:T(8,128)} copy(f32[128,1,6,128]{0,3,2,1:T(8,128)} %get-tuple-element.296) | data formatting | bytes 786432 | tf_op jit(solution)/shard_map/slice | solution.py:44
  28.9 1.9 %copy.39 = f32[128,1,6,128]{3,0,2,1:T(8,128)} copy(f32[128,1,6,128]{0,3,2,1:T(8,128)} %get-tuple-element.295) | data formatting | bytes 786432 | tf_op jit(solution)/shard_map/slice | solution.py:45
  30.9 1.1 fusion.50
  33.3 1.3 rsqrt.36
  34.7 1.9 %copy.41 = f32[128,1,6,128]{3,0,2,1:T(8,128)} copy(f32[128,1,6,128]{0,3,2,1:T(8,128)} %get-tuple-element.294) | data formatting | bytes 786432 | tf_op jit(solution)/shard_map/slice | solution.py:43
  36.6 1.2 multiply_bitcast_fusion
  38.9 1.5 convolution_select_fusion
  47.4 1.0 fusion.66
  49.1 16.6 %while.38 = (s32[]{:T(128)}, f32[6,128,256]{2,1,0:T(8,128)}, f32[2,6,64,128]{3,2,1,0:T(8,128)}, f32[2,6,64,128]{3,2,1,0:T(8,128)}, f32[2,6,64,128]{3,2,1,0:T(8,1...) while((s32[]{:T(128)}, f32[6,128,256]{2,1,0:T(8,128)}, ...), condition=%wide.region_3.4_spmd, body=%wide.region_2.3_spmd.sunk | while | flops 415678464 | bytes 10029241 | solution.py:119
  49.1 1.9 %fusion.137 = f32[6,64,256]{2,1,0:T(8,128)S(1)} fusion(f32[6,128,256]{2,1,0:T(8,128)} %get-tuple-element.445, f32[2,6,64,128]{3,2,1,0:T(8,128)} %get-tuple-element.457, s32[]{:T(128)} %get-tuple-element.444), kind=kOutput, calls=%fused_computation.13.clone.1 | convolution fusion | flops 150994944 | bytes 1376768 | tf_op jit(solution)/shard_map/while/body/eval_jaxpr/rnf,rfw->rnw/dot_general | solution.py:104
  51.0 1.0 slice_negate_fusion.2
  52.0 1.5 fusion.138
  53.5 2.9 %convolution_add_fusion.10 = f32[6,128,256]{2,1,0:T(8,128)} fusion(f32[6,128,256]{2,1,0:T(8,128)} %get-tuple-element.445, f32[6,64,128]{2,1,0:T(8,128)S(1)} %get-tuple-element.421, f32[6,64,128]{2,1,0:T(8,128)S(1)} %get-tuple-element.422, f32[2,6,64,128]{3,2,1,0:T(8,128)S(1)} %copy-done.2, s32[]{:T(128)} %get-tuple-element.444), kind=kOutput, calls=%fused_computation.clone.1 | convolution fusion | flops 151289856 | bytes 2162692 | tf_op jit(solution)/shard_map/while/body/eval_jaxpr/mjr,mjz->mrz/dot_general | solution.py:113
  56.4 1.0 fusion.139
  57.4 1.9 %fusion.137 = f32[6,64,256]{2,1,0:T(8,128)S(1)} fusion(f32[6,128,256]{2,1,0:T(8,128)} %get-tuple-element.445, f32[2,6,64,128]{3,2,1,0:T(8,128)} %get-tuple-element.457, s32[]{:T(128)} %get-tuple-element.444), kind=kOutput, calls=%fused_computation.13.clone.1 | convolution fusion | flops 150994944 | bytes 1376768 | tf_op jit(solution)/shard_map/while/body/eval_jaxpr/rnf,rfw->rnw/dot_general | solution.py:104
  59.3 1.0 slice_negate_fusion.2
  60.3 1.5 fusion.138
  61.8 2.9 %convolution_add_fusion.10 = f32[6,128,256]{2,1,0:T(8,128)} fusion(f32[6,128,256]{2,1,0:T(8,128)} %get-tuple-element.445, f32[6,64,128]{2,1,0:T(8,128)S(1)} %get-tuple-element.421, f32[6,64,128]{2,1,0:T(8,128)S(1)} %get-tuple-element.422, f32[2,6,64,128]{3,2,1,0:T(8,128)S(1)} %copy-done.2, s32[]{:T(128)} %get-tuple-element.444), kind=kOutput, calls=%fused_computation.clone.1 | convolution fusion | flops 151289856 | bytes 2162692 | tf_op jit(solution)/shard_map/while/body/eval_jaxpr/mjr,mjz->mrz/dot_general | solution.py:113
  64.7 1.0 fusion.139
  65.7 2.1 %fusion.65 = (f32[6,128,128]{2,1,0:T(8,128)}, f32[6,128,128]{2,1,0:T(8,128)}) fusion(f32[6,128,256]{2,1,0:T(8,128)} %get-tuple-element.180), kind=kLoop, calls=%fused_computation.102 | loop fusion | bytes 1572864 | tf_op jit(solution)/shard_map/slice | solution.py:121
  68.6 31.2 %all-gather.5.cloned.1.call-done = f32[24,128,128]{2,1,0:T(8,128)} async-done(((f32[6,128,128]{2,1,0:T(8,128)}), f32[24,128,128]{2,1,0:T(8,128)}) %all-gather.5.cloned.1.call-update) | async-done | bytes 1572880 | tf_op jit(solution)/shard_map/all_gather | solution.py:14
  99.8 32.7 %all-gather.7.cloned.1.call-done = f32[24,128,128]{2,1,0:T(8,128)} async-done(((f32[6,128,128]{2,1,0:T(8,128)}), f32[24,128,128]{2,1,0:T(8,128)}) %all-gather.7.cloned.1.call-update) | async-done | bytes 1572880 | tf_op jit(solution)/shard_map/all_gather | solution.py:14
  132.5 10.2 %while.40 = (s32[]{:T(128)}, f32[6,128,128]{2,1,0:T(8,128)}, s32[]{:T(128)}, f32[4,6,128,128]{3,2,1,0:T(8,128)}, f32[4,6,128,128]{3,2,1,0:T(8,128)}, /*index=5*/s32[]{:T(128)}, s32[]{:T(128)}) while((s32[]{:T(128)}, f32[6,128,128]{2,1,0:T(8,128)}, s32[]{:T(128)}, f32[4,6,128,128]{3,2,1,0:T(8,128)}, f32[4,6,128,128]{3,2,1,0:T(8,128)}, ...), condition=%wide.region_5.6_spmd.clone, body=%wide.region_4.5_spmd.clone.sunk | while | flops 151388160 | bytes 2755167 | solution.py:23
  132.5 1.0 copy.87
  133.5 2.4 %fusion.153 = f32[6,128,128]{2,1,0:T(8,128)} fusion(f32[6,128,128]{2,1,0:T(8,128)S(1)} %copy.87, f32[4,6,128,128]{3,2,1,0:T(8,128)} %get-tuple-element.480, s32[]{:T(128)} %get-tuple-element.469, f32[4,6,128,128]{3,2,1,0:T(8,128)} %get-tuple-element.479, pred[]{:T(512)S(6)} %compare.4, pred[]{:T(512)S(6)} %lt.30), kind=kOutput, calls=%fused_computation.44.clone.1 | convolution fusion | flops 151388160 | bytes 1968640 | tf_op jit(solution)/shard_map/while/body/eval_jaxpr/hij,hjk->hik/dot_general | solution.py:80
  135.9 1.0 copy.87
  136.9 2.4 %fusion.153 = f32[6,128,128]{2,1,0:T(8,128)} fusion(f32[6,128,128]{2,1,0:T(8,128)S(1)} %copy.87, f32[4,6,128,128]{3,2,1,0:T(8,128)} %get-tuple-element.480, s32[]{:T(128)} %get-tuple-element.469, f32[4,6,128,128]{3,2,1,0:T(8,128)} %get-tuple-element.479, pred[]{:T(512)S(6)} %compare.4, pred[]{:T(512)S(6)} %lt.30), kind=kOutput, calls=%fused_computation.44.clone.1 | convolution fusion | flops 151388160 | bytes 1968640 | tf_op jit(solution)/shard_map/while/body/eval_jaxpr/hij,hjk->hik/dot_general | solution.py:80
  139.3 1.0 copy.87
  140.3 2.4 %fusion.153 = f32[6,128,128]{2,1,0:T(8,128)} fusion(f32[6,128,128]{2,1,0:T(8,128)S(1)} %copy.87, f32[4,6,128,128]{3,2,1,0:T(8,128)} %get-tuple-element.480, s32[]{:T(128)} %get-tuple-element.469, f32[4,6,128,128]{3,2,1,0:T(8,128)} %get-tuple-element.479, pred[]{:T(512)S(6)} %compare.4, pred[]{:T(512)S(6)} %lt.30), kind=kOutput, calls=%fused_computation.44.clone.1 | convolution fusion | flops 151388160 | bytes 1968640 | tf_op jit(solution)/shard_map/while/body/eval_jaxpr/hij,hjk->hik/dot_general | solution.py:80
  143.5 13.9 %while.39 = (s32[]{:T(128)}, f32[6,128,128]{2,1,0:T(8,128)}, f32[2,6,64,128]{3,2,1,0:T(8,128)}, f32[2,6,64,128]{3,2,1,0:T(8,128)}, f32[2,6,64,128]{3,2,1,0:T(8,1...) while((s32[]{:T(128)}, f32[6,128,128]{2,1,0:T(8,128)}, ...), condition=%wide.region_7.8_spmd, body=%wide.region_6.7_spmd.sunk | while | flops 264388608 | bytes 9046217 | solution.py:138
  143.6 1.6 fusion.148
  145.2 1.6 fusion.149
  147.9 2.6 %convolution_subtract_fusion.3 = f32[6,128,128]{2,1,0:T(8,128)} fusion(f32[6,128,128]{2,1,0:T(8,128)} %get-tuple-element.492, f32[6,64,128]{2,1,0:T(8,128)S(1)} %fusion.148, f32[2,6,64,128]{3,2,1,0:T(8,128)S(1)} %copy-done.3, s32[]{:T(128)} %get-tuple-element.491), kind=kOutput, calls=%fused_computation.25.clone.1 | convolution fusion | flops 75595776 | bytes 1179652 | tf_op jit(solution)/shard_map/while/body/eval_jaxpr/mjr,mjz->mrz/dot_general | solution.py:133
  150.5 1.6 fusion.148
  152.1 1.6 fusion.149
  154.8 2.6 %convolution_subtract_fusion.3 = f32[6,128,128]{2,1,0:T(8,128)} fusion(f32[6,128,128]{2,1,0:T(8,128)} %get-tuple-element.492, f32[6,64,128]{2,1,0:T(8,128)S(1)} %fusion.148, f32[2,6,64,128]{3,2,1,0:T(8,128)S(1)} %copy-done.3, s32[]{:T(128)} %get-tuple-element.491), kind=kOutput, calls=%fused_computation.25.clone.1 | convolution fusion | flops 75595776 | bytes 1179652 | tf_op jit(solution)/shard_map/while/body/eval_jaxpr/mjr,mjz->mrz/dot_general | solution.py:133
  157.4 2.0 %multiply_reduce_fusion = (f32[2,64,6]{1,2,0:T(8,128)S(1)}, f32[2,64,6,128]{3,1,2,0:T(8,128)}) fusion(f32[2,6,64,128]{3,2,1,0:T(8,128)} %get-tuple-element.179, f32[2,6,64,128]{3,2,1,0:T(8,128)} %get-tuple-element.182), kind=kLoop, calls=%fused_computation.77 | loop fusion | flops 294144 | bytes 1182720 | tf_op jit(solution)/shard_map/reduce_sum | solution.py:70
  160.2 1.9 %copy.47 = f32[128,768]{1,0:T(8,128)} copy(f32[128,768]{0,1:T(8,128)} %bitcast.157) | data formatting | bytes 786432 | tf_op jit(solution)/shard_map/mul | solution.py:71
  162.1 1.2 copy.45
  163.4 1.8 %fusion.56 = bf16[128,768]{1,0:T(8,128)(2,1)} fusion(f32[128,768]{1,0:T(8,128)} %copy.47, f32[16,8,6,128]{3,2,1,0:T(8,128)S(1)} %bitcast.155, f32[768]{0:T(1024)S(1)} %copy-done.14), kind=kLoop, calls=%fused_computation.73 | loop fusion | flops 294912 | bytes 986112 | tf_op jit(solution)/shard_map/convert_element_type | solution.py:72
  (82 shorter events, 18.6 us)
Async XLA Ops:
  6.5 12.2 %copy-start = (bf16[768,2304]{1,0:T(8,128)(2,1)S(1)}, bf16[768,2304]{1,0:T(8,128)(2,1)}, u32[]{:S(2)}) copy-start(bf16[768,2304]{1,0:T(8,128)(2,1)} %param.12) | copy-start | bytes 10616836
  8.3 10.5 %all-to-all-start = ((bf16[4,192,128]{2,1,0:T(8,128)(2,1)}), bf16[4,192,128]{2,1,0:T(8,128)(2,1)}, u32[]{:S(2)}, u32[]{:S(2)}) async-start(bf16[4,192,128]{2,1,0:T(8,128)(2,1)} %pad_maximum_fusion), calls=%async_computation | async-start | bytes 393216 | tf_op jit(solution)/shard_map/all_to_all | solution.py:88
  13.5 86.3 %all-gather.5.cloned.1.call-start = ((), (), s32[]{:S(2)}) async-start(), calls=%async_computation.1 | async-start | bytes 1966080 | tf_op jit(solution)/shard_map/all_gather | solution.py:14
  36.6 2.0 %copy-start.9 = (f32[128,1,6,128]{3,0,2,1:T(8,128)S(1)}, f32[128,1,6,128]{3,0,2,1:T(8,128)}, u32[]{:S(2)}) copy-start(f32[128,1,6,128]{3,0,2,1:T(8,128)} %copy.35) | copy-start | bytes 1179652
  36.6 2.0 %copy-start.10 = (f32[128,1,6,128]{3,0,2,1:T(8,128)S(1)}, f32[128,1,6,128]{3,0,2,1:T(8,128)}, u32[]{:S(2)}) copy-start(f32[128,1,6,128]{3,0,2,1:T(8,128)} %copy.39) | copy-start | bytes 1179652
  37.8 1.1 copy-start.13
  38.6 1.8 %copy-start.12 = (pred[64,64]{1,0:T(8,128)(4,1)S(1)}, pred[64,64]{1,0:T(8,128)(4,1)}, u32[]{:S(2)}) copy-start(pred[64,64]{1,0:T(8,128)(4,1)} %iota_compare_fusion.2) | copy-start | bytes 12292
  38.9 2.9 %copy-start.1 = (f32[2,6,64,128]{3,2,1,0:T(8,128)}, f32[2,6,64,128]{3,2,1,0:T(8,128)S(1)}, u32[]{:S(2)}) copy-start(f32[2,6,64,128]{3,2,1,0:T(8,128)S(1)} %get-tuple-element.486) | copy-start | bytes 1179652
  40.4 1.9 %copy-start.11 = (f32[64,64]{1,0:T(8,128)S(1)}, f32[64,64]{1,0:T(8,128)}, u32[]{:S(2)}) copy-start(f32[64,64]{1,0:T(8,128)} %fusion.61) | copy-start | bytes 49156
  49.1 2.9 %copy-start.4 = (f32[2,6,64,128]{3,2,1,0:T(8,128)S(1)}, f32[2,6,64,128]{3,2,1,0:T(8,128)}, u32[]{:S(2)}) copy-start(f32[2,6,64,128]{3,2,1,0:T(8,128)} %get-tuple-element.459) | copy-start | bytes 1179652 | tf_op jit(solution)/shard_map/while
  49.1 4.4 %copy-start.2 = (f32[2,6,64,128]{3,2,1,0:T(8,128)S(1)}, f32[2,6,64,128]{3,2,1,0:T(8,128)}, u32[]{:S(2)}) copy-start(f32[2,6,64,128]{3,2,1,0:T(8,128)} %get-tuple-element.456) | copy-start | bytes 1179652 | tf_op jit(solution)/shard_map/while
  52.0 4.4 %copy-start.5 = (f32[2,6,64,64]{3,2,1,0:T(8,128)S(1)}, f32[2,6,64,64]{3,2,1,0:T(8,128)}, u32[]{:S(2)}) copy-start(f32[2,6,64,64]{3,2,1,0:T(8,128)} %get-tuple-element.460) | copy-start | bytes 589828 | tf_op jit(solution)/shard_map/while
  57.4 2.9 %copy-start.4 = (f32[2,6,64,128]{3,2,1,0:T(8,128)S(1)}, f32[2,6,64,128]{3,2,1,0:T(8,128)}, u32[]{:S(2)}) copy-start(f32[2,6,64,128]{3,2,1,0:T(8,128)} %get-tuple-element.459) | copy-start | bytes 1179652 | tf_op jit(solution)/shard_map/while
  57.4 4.4 %copy-start.2 = (f32[2,6,64,128]{3,2,1,0:T(8,128)S(1)}, f32[2,6,64,128]{3,2,1,0:T(8,128)}, u32[]{:S(2)}) copy-start(f32[2,6,64,128]{3,2,1,0:T(8,128)} %get-tuple-element.456) | copy-start | bytes 1179652 | tf_op jit(solution)/shard_map/while
  60.3 4.4 %copy-start.5 = (f32[2,6,64,64]{3,2,1,0:T(8,128)S(1)}, f32[2,6,64,64]{3,2,1,0:T(8,128)}, u32[]{:S(2)}) copy-start(f32[2,6,64,64]{3,2,1,0:T(8,128)} %get-tuple-element.460) | copy-start | bytes 589828 | tf_op jit(solution)/shard_map/while
  67.8 64.7 %all-gather.7.cloned.1.call-start = ((), (), s32[]{:S(2)}) async-start(), calls=%async_computation.2 | async-start | bytes 1966080 | tf_op jit(solution)/shard_map/all_gather | solution.py:14
  143.5 3.2 %copy-start.6 = (f32[2,6,64,64]{3,2,1,0:T(8,128)S(1)}, f32[2,6,64,64]{3,2,1,0:T(8,128)}, u32[]{:S(2)}) copy-start(f32[2,6,64,64]{3,2,1,0:T(8,128)} %get-tuple-element.505) | copy-start | bytes 589828 | tf_op jit(solution)/shard_map/while
  143.5 3.3 %copy-start.7 = (f32[2,6,64,128]{3,2,1,0:T(8,128)S(1)}, f32[2,6,64,128]{3,2,1,0:T(8,128)}, u32[]{:S(2)}) copy-start(f32[2,6,64,128]{3,2,1,0:T(8,128)} %get-tuple-element.493) | copy-start | bytes 1179652 | tf_op jit(solution)/shard_map/while
  143.6 4.4 %copy-start.3 = (f32[2,6,64,128]{3,2,1,0:T(8,128)S(1)}, f32[2,6,64,128]{3,2,1,0:T(8,128)}, u32[]{:S(2)}) copy-start(f32[2,6,64,128]{3,2,1,0:T(8,128)} %get-tuple-element.502) | copy-start | bytes 1179652 | tf_op jit(solution)/shard_map/while
  147.1 0.8 copy-start.8
  150.5 3.2 %copy-start.6 = (f32[2,6,64,64]{3,2,1,0:T(8,128)S(1)}, f32[2,6,64,64]{3,2,1,0:T(8,128)}, u32[]{:S(2)}) copy-start(f32[2,6,64,64]{3,2,1,0:T(8,128)} %get-tuple-element.505) | copy-start | bytes 589828 | tf_op jit(solution)/shard_map/while
  150.5 3.3 %copy-start.7 = (f32[2,6,64,128]{3,2,1,0:T(8,128)S(1)}, f32[2,6,64,128]{3,2,1,0:T(8,128)}, u32[]{:S(2)}) copy-start(f32[2,6,64,128]{3,2,1,0:T(8,128)} %get-tuple-element.493) | copy-start | bytes 1179652 | tf_op jit(solution)/shard_map/while
  150.5 4.4 %copy-start.3 = (f32[2,6,64,128]{3,2,1,0:T(8,128)S(1)}, f32[2,6,64,128]{3,2,1,0:T(8,128)}, u32[]{:S(2)}) copy-start(f32[2,6,64,128]{3,2,1,0:T(8,128)} %get-tuple-element.502) | copy-start | bytes 1179652 | tf_op jit(solution)/shard_map/while
  154.1 0.8 copy-start.8
  157.4 6.0 %copy-start.14 = (f32[768]{0:T(1024)S(1)}, f32[768]{0:T(1024)}, u32[]{:S(2)}) copy-start(f32[768]{0:T(1024)} %param.15) | copy-start | bytes 9220
Sparse Core Ops, SparseCore 0:
  67.9 31.8 all-gather.4
  101.7 30.8 all-gather.6
